TPU v7x, 256 devices: a whole 4x4x8 slice. The times are simulated.
256 devices in a mesh: gx: 64 (over z, x, core), gy: 4 (over y).
Axes of the slice: x: 4, y: 4, z: 8, core: 2. Of those that a mesh axis runs over, the one named last changes fastest.
Arguments:
- volume: bfloat16 [128, 16, 128, 256], P('gx', 'gy'), may hold values from -40 to 40
- void_mask: int32 [128, 16, 128], P('gx', 'gy'), may hold values from 0 to 1, as said below
- kernel: bfloat16 [27, 256], replicated, may hold values from -1.25 to 1.25
- mix_weight: bfloat16 [4, 64, 64], replicated, may hold values from -0.75 to 0.75
- norm_gain: float32 [256], replicated, may hold values from 0.25 to 1.75
- upstream: bfloat16 [128, 16, 128, 256], P('gx', 'gy'), may hold values from -6 to 6
Outputs:
- output: bfloat16 [128, 16, 128, 256], P('gx', 'gy')
- volume_grad: bfloat16 [128, 16, 128, 256], P('gx', 'gy')
- kernel_grad: float32 [27, 256], replicated
- mix_grad: float32 [4, 64, 64], replicated
Inputs may be any that keep to these rules, and one draw needn't show every extreme that they name: `void_mask`: 1 marks a void voxel; voxels whose third index is a multiple of 8 are never void.
All inputs are finite; a program needn't handle non-finite values.
Results may differ from a plain program's by a relative error of at most 0.0017.
The roundings to bfloat16 on the way count: a program that leaves them out, or rounds other values in their place, can miss the bound.
Values may be sent and summed in bfloat16 or wider, within the bound.
No kernel may reach another device: no remote copies, remote signals or barrier semaphores. Data moves between devices by JAX's collectives and lax.ppermute only.
A program may use at most 128 MiB of HBM per device.

v0:
```python
import jax
import jax.numpy as jnp
from jax import lax
from jax.sharding import PartitionSpec as P

SWEEPS = 5
HI = lax.Precision.HIGHEST
EPS = 1e-05


def padded_2(block, sides, width):
    for axis, dim in sides:
        count = lax.axis_size(axis)
        forward = [(i, i + 1) for i in range(count - 1)]
        forward.append((count - 1, 0))
        backward = [(target, source) for source, target in forward]
        low = lax.ppermute(
            lax.slice_in_dim(block, block.shape[dim] - width, None, axis=dim), axis, forward
        )
        high = lax.ppermute(lax.slice_in_dim(block, 0, width, axis=dim), axis, backward)
        block = jnp.concatenate([low, block, high], axis=dim)
    return block


def whiten(sigma):
    eye = jnp.eye(sigma.shape[0], dtype=sigma.dtype)
    trace = jnp.trace(sigma)
    scaled = sigma / trace
    proj = eye
    for sweep in range(SWEEPS):
        cube = jnp.dot(
            proj, jnp.dot(proj, jnp.dot(proj, scaled, precision=HI), precision=HI), precision=HI
        )
        proj = 1.5 * proj - 0.5 * cube
    return proj / jnp.sqrt(trace)


def sigma_back(sigma, dwhite):
    return jax.vjp(whiten, sigma)[1](dwhite)[0]


def zwrap(field):
    return jnp.concatenate([field[:, :, -1:], field, field[:, :, :1]], axis=2)


def stencil(padded, kernel, flip):
    size_x, size_y, depth = (padded.shape[0] - 2, padded.shape[1] - 2, padded.shape[2] - 2)
    taps = kernel.astype(jnp.float32)
    total = jnp.zeros((size_x, size_y, depth, padded.shape[3]), jnp.float32)
    for tap in range(27):
        ox, oy, oz = (tap // 9, tap // 3 % 3, tap % 3)
        if flip:
            ox, oy, oz = (2 - ox, 2 - oy, 2 - oz)
        piece = padded[ox : ox + size_x, oy : oy + size_y, oz : oz + depth]
        total = total + piece.astype(jnp.float32) * taps[tap]
    return total


def inner(field, edge):
    return field[edge : field.shape[0] - edge, edge : field.shape[1] - edge]


def per_device(volume, void_mask, kernel, mix_weight, norm_gain, upstream):
    size_x, size_y, depth, chans = volume.shape
    groups, width = (mix_weight.shape[0], mix_weight.shape[1])
    scale = jnp.float32(size_x * size_y * depth * lax.axis_size("gx") * lax.axis_size("gy"))
    keep_own = (1 - void_mask).astype(jnp.float32)
    rim = 1
    padded_x = padded_2(volume, (("gx", 0), ("gy", 1)), 1)
    edge = rim - 1
    padded_z = zwrap(padded_x)
    field = lax.optimization_barrier(stencil(padded_z, kernel, False).astype(jnp.bfloat16)).astype(
        jnp.float32
    )
    ext_x, ext_y = (field.shape[0], field.shape[1])
    field_own = inner(field, edge)
    masked_own = keep_own[..., None] * field_own
    count_part = jnp.sum(keep_own)
    sum_part = jnp.sum(masked_own, axis=(0, 1, 2))
    eye = jnp.eye(width, dtype=jnp.float32)
    count, total = lax.psum((count_part, sum_part), ("gx", "gy"))
    mean = (total / count).reshape(groups, width)
    cent_own = field_own.reshape(size_x, size_y, depth, groups, width) - mean
    cov_part = jnp.einsum(
        "abzgi,abzgj->gij", keep_own[..., None, None] * cent_own, cent_own, precision=HI
    )
    sigma = lax.psum(cov_part, ("gx", "gy")) / count + EPS * eye
    white = jax.vmap(whiten)(sigma)
    centered = field.reshape(ext_x, ext_y, depth, groups, width) - mean
    gain = norm_gain.reshape(groups, width)
    pre = jnp.einsum("abzgj,gij->abzgi", centered, white, precision=HI) * gain
    active = jax.nn.silu(pre).astype(jnp.bfloat16)
    active_own = inner(active, edge)
    grad_five = upstream.reshape(ext_x, ext_y, depth, groups, width)
    mixed = jnp.einsum(
        "abzgi,gio->abzgo", active_own, mix_weight, preferred_element_type=jnp.float32
    )
    output = (volume.astype(jnp.float32) + mixed.reshape(size_x, size_y, depth, chans)).astype(
        jnp.bfloat16
    )
    dact = jnp.einsum("abzgo,gio->abzgi", grad_five, mix_weight, preferred_element_type=jnp.float32)
    sig = jax.nn.sigmoid(pre)
    dnormed = dact * sig * (1.0 + pre * (1.0 - sig)) * gain
    dcent = jnp.einsum("abzgi,gij->abzgj", dnormed, white, precision=HI)
    dwhite_part = jnp.einsum(
        "abzgi,abzgj->gij", inner(dnormed, edge), inner(centered, edge), precision=HI
    )
    dsum_part = jnp.sum(inner(dcent, edge), axis=(0, 1, 2))
    dwhite, dsum = lax.psum((dwhite_part, dsum_part), ("gx", "gy"))
    sens = jax.vmap(sigma_back)(sigma, dwhite)
    sym = sens + jnp.swapaxes(sens, 1, 2)
    dfield = dcent + keep_own[..., None, None] / count * (
        jnp.einsum("abzgj,gjk->abzgk", centered, sym, precision=HI) - dsum
    )
    dfield = lax.optimization_barrier(
        dfield.astype(jnp.bfloat16).reshape(ext_x, ext_y, depth, chans)
    )
    dfield_pad = zwrap(padded_2(dfield, (("gx", 0), ("gy", 1)), 1))
    back = stencil(dfield_pad, kernel, True)
    volume_grad = (upstream.astype(jnp.float32) + back).astype(jnp.bfloat16)
    dfield_own = inner(dfield, edge).astype(jnp.float32)
    ker_terms = []
    for tap in range(27):
        ox, oy, oz = (tap // 9, tap // 3 % 3, tap % 3)
        piece = padded_z[
            edge + ox : edge + ox + size_x, edge + oy : edge + oy + size_y, oz : oz + depth
        ]
        ker_terms.append(jnp.sum(piece.astype(jnp.float32) * dfield_own, axis=(0, 1, 2)))
    ker_part = jnp.stack(ker_terms)
    mix_part = jnp.einsum(
        "abzgi,abzgo->gio",
        active_own,
        upstream.reshape(size_x, size_y, depth, groups, width),
        preferred_element_type=jnp.float32,
    )
    ker_sum, mix_sum = lax.psum((ker_part, mix_part), ("gx", "gy"))
    return (output, volume_grad, ker_sum / scale, mix_sum / scale)


def solution(mesh):
    in_specs = (
        P("gx", "gy", None, None),
        P("gx", "gy", None),
        P(),
        P(),
        P(),
        P("gx", "gy", None, None),
    )
    out_specs = (P("gx", "gy", None, None), P("gx", "gy", None, None), P(), P())
    return jax.shard_map(
        per_device, mesh=mesh, in_specs=in_specs, out_specs=out_specs, check_vma=False
    )
```

profile of v0, /device:TPU:32, one launch (start us, length us, event | category | flops | bytes accessed | tf_op | source)
XLA Modules:
  0.0 774.9 jit_solution(11708608485674876713)
XLA Ops:
  7.3 1.4 copy.36
  8.8 3.8 collective-permute-start.1
  12.7 0.7 subtract_convert_fusion
  14.0 1.5 fusion.156
  15.5 1.2 collective-permute-done
  16.8 1.7 collective-permute-start.2
  18.4 1.7 collective-permute-start.3
  20.7 0.7 mul.785
  21.4 1.1 copy.47
  22.6 3.5 collective-permute-done.2
  26.4 0.7 fusion.152
  27.5 5.9 maximum_maximum_fusion
  33.7 4.6 fusion.47
  38.3 0.8 copy-done.17
  39.3 79.1 %all-reduce = (f32[256]{0:T(256)S(1)}, f32[]{:T(128)}) all-reduce(f32[256]{0:T(256)S(1)} %multiply_reduce_fusion, f32[]{:T(128)} %fusion.150), channel_id=1, replica_groups=mesh['gx'=64,'gy'=4] {'gx','gy'}, use_global_device_ids=true, to_apply=%region_1.0 | all-reduce | flops 257 | bytes 2056 | tf_op jit(solution)/shard_map/psum | solution.py:81
  118.4 0.6 broadcast_divide_fusion.8
  119.1 3.2 fusion.10
  122.8 1.2 broadcast_divide_fusion.7
  124.1 235.6 %all-reduce.5.cloned.1.call-done = f32[4,64,64]{2,1,0:T(8,128)} async-done(((f32[4,64,64]{2,1,0:T(8,128)}), f32[4,64,64]{2,1,0:T(8,128)}) %all-reduce.5.cloned.1.call-update) | async-done | bytes 65552 | tf_op jit(solution)/shard_map/psum | solution.py:87
  359.7 1.7 select_reduce_fusion
  362.0 1.6 broadcast_divide_fusion.2
  364.5 0.6 copy-done.37
  367.0 0.6 copy-done.40
  369.2 2.0 multiply_convert_fusion
  371.8 1.8 convolution_bitcast_fusion.6
  373.6 2.1 fusion.157
  375.7 0.9 convolution_bitcast_fusion.3
  376.7 1.4 convolution_bitcast_fusion.1
  378.1 1.1 copy.46
  379.2 76.3 %psum.53 = f32[4,64]{1,0:T(4,128)S(1)} all-reduce(f32[4,64]{1,0:T(4,128)S(1)} %get-tuple-element.105), channel_id=1, replica_groups=mesh['gx'=64,'gy'=4] {'gx','gy'}, use_global_device_ids=true, to_apply=%region_10.11 | all-reduce | flops 256 | bytes 2048 | tf_op jit(solution)/shard_map/psum | solution.py:109
  455.5 168.1 %all-reduce.7.cloned.1.call-done = (f32[4,64,64]{2,1,0:T(8,128)}, f32[4,64,64]{2,1,0:T(8,128)}) async-done(((f32[4,64,64]{2,1,0:T(8,128)}, f32[4,64,64]{2,1,0:T(8,128)}), (f32[4,64,64]{2,1,0:T(8,128)}, f32[4,64,64]{2,1,0:T(8,128)})) %all-reduce.7.cloned.1.call-update) | async-done | bytes 131088 | tf_op jit(solution)/shard_map/psum | solution.py:109
  623.6 1.5 fusion.114
  625.1 1.5 convolution_add_fusion.14
  626.5 1.2 fusion.166
  627.7 1.2 fusion.167
  628.9 1.3 convolution_add_fusion.13
  634.8 1.0 convolution_add_fusion.2
  636.6 0.6 copy-done.44
  637.3 0.9 convolution_add_fusion.3
  638.2 1.7 copy.71
  639.8 1.4 convolution_add_fusion.1
  641.3 1.3 fusion.16
  643.1 0.9 fusion.130
  643.9 1.7 copy.70
  645.6 2.5 multiply_reduce_fusion.1
  648.2 2.9 fusion.9
  651.2 0.9 fusion.153
  652.1 0.7 collective-permute-start.4
  652.8 3.4 collective-permute-start.5
  656.2 4.8 fusion.90
  661.0 1.5 fusion.89
  662.6 78.1 %psum.54 = f32[27,256]{1,0:T(8,128)S(1)} all-reduce(f32[27,256]{1,0:T(8,128)S(1)} %stack.111), channel_id=1, replica_groups=mesh['gx'=64,'gy'=4] {'gx','gy'}, use_global_device_ids=true, to_apply=%region_38.39 | all-reduce | flops 6912 | bytes 55296 | tf_op jit(solution)/shard_map/psum | solution.py:136
  740.7 1.1 pad_maximum_fusion.12
  741.9 3.2 collective-permute-start.7
  745.2 0.6 broadcast_multiply_fusion.1
  745.8 2.0 copy.76
  747.8 1.6 broadcast_multiply_fusion
  749.4 1.3 collective-permute-done.6
  750.7 1.4 pad_maximum_fusion.3
  752.0 0.7 fusion.151
  752.8 1.6 pad_maximum_fusion.5
  754.6 4.6 pad_maximum_fusion.1
  759.5 6.3 fusion.93
  765.8 2.0 copy.77
  (286 shorter events, 14.2 us)
Async XLA Ops:
  7.2 364.1 %copy-start = (bf16[4,64,64]{2,1,0:T(8,128)(2,1)S(1)}, bf16[4,64,64]{2,1,0:T(8,128)(2,1)}, u32[]{:S(2)}) copy-start(bf16[4,64,64]{2,1,0:T(8,128)(2,1)} %param.9) | copy-start | bytes 98308
  7.2 12.9 %copy-start.49 = (s32[2,4,128]{2,1,0:T(4,128)S(1)}, s32[2,4,128]{2,1,0:T(4,128)}, u32[]{:S(2)}) copy-start(s32[2,4,128]{2,1,0:T(4,128)} %param.7) | copy-start | bytes 12292
  7.2 15.2 %copy-start.48 = (bf16[27,256]{1,0:T(8,128)(2,1)S(1)}, bf16[27,256]{1,0:T(8,128)(2,1)}, u32[]{:S(2)}) copy-start(bf16[27,256]{1,0:T(8,128)(2,1)} %param.8) | copy-start | bytes 41476
  7.2 13.5 %copy-start.114 = (f32[256]{0:T(256)S(1)}, f32[256]{0:T(256)}, u32[]{:S(2)}) copy-start(f32[256]{0:T(256)} %param.10) | copy-start | bytes 3076
  7.2 14.1 %copy-start.47 = (bf16[2,4,128,256]{3,2,1,0:T(8,128)(2,1)S(1)}, bf16[2,4,128,256]{3,2,1,0:T(8,128)(2,1)}, u32[]{:S(2)}) copy-start(bf16[2,4,128,256]{3,2,1,0:T(8,128)(2,1)} %param.11) | copy-start | bytes 1572868
  7.2 352.5 %all-reduce.5.cloned.1.call-start = ((), (), s32[]{:S(2)}) async-start(), calls=%async_computation | async-start | bytes 262144 | tf_op jit(solution)/shard_map/psum | solution.py:87
  8.7 18.4 %copy-start.5 = (bf16[2,4,128,256]{2,3,1,0:T(8,128)(2,1)}, bf16[2,4,128,256]{2,3,1,0:T(8,128)(2,1)S(1)}, u32[]{:S(2)}) copy-start(bf16[2,4,128,256]{2,3,1,0:T(8,128)(2,1)S(1)} %copy.36) | copy-start | bytes 1572868
  8.7 8.0 %collective-permute-start = (bf16[1,4,128,256]{2,3,1,0:T(8,128)(2,1)S(1)}, bf16[1,4,128,256]{2,3,1,0:T(8,128)(2,1)S(1)}, u32[]{:S(2)}, u32[]{:S(2)}) collective-permute-start(bf16[1,4,128,256]{2,3,1,0:T(8,128)(2,1)S(1)} %get-tuple-element.74), channel_id=1, source_target_pairs={{0,4},{4,8},{8,12},{12,16},{16,20},{20,24},{24,28},{28,32},{32,36}... | collective-permute-start | bytes 786440 | tf_op jit(solution)/shard_map/ppermute | solution.py:17
  8.8 7.9 %collective-permute-start.1 = (bf16[1,4,128,256]{2,3,1,0:T(8,128)(2,1)S(1)}, bf16[1,4,128,256]{2,3,1,0:T(8,128)(2,1)S(1)}, u32[]{:S(2)}, u32[]{:S(2)}) collective-permute-start(bf16[1,4,128,256]{2,3,1,0:T(8,128)(2,1)S(1)} %get-tuple-element.73), channel_id=1, source_target_pairs={{4,0},{8,4},{12,8},{16,12},{20,16},{24,20},{28,24},{32,28},{36,32}... | collective-permute-start | bytes 786440 | tf_op jit(solution)/shard_map/ppermute | solution.py:20
  13.4 24.9 %copy-start.52 = (f32[2,4,128]{2,1,0:T(4,128)}, f32[2,4,128]{2,1,0:T(4,128)S(1)}, u32[]{:S(2)}) copy-start(f32[2,4,128]{2,1,0:T(4,128)S(1)} %subtract_convert_fusion) | copy-start | bytes 12292
  16.7 16.7 %copy-start.12 = (bf16[1,4,128,256]{2,3,1,0:T(8,128)(2,1)}, bf16[1,4,128,256]{2,3,1,0:T(8,128)(2,1)S(1)}, u32[]{:S(2)}) copy-start(bf16[1,4,128,256]{2,3,1,0:T(8,128)(2,1)S(1)} %collective-permute-done) | copy-start | bytes 786436
  16.7 10.4 %copy-start.14 = (bf16[1,4,128,256]{2,3,1,0:T(8,128)(2,1)}, bf16[1,4,128,256]{2,3,1,0:T(8,128)(2,1)S(1)}, u32[]{:S(2)}) copy-start(bf16[1,4,128,256]{2,3,1,0:T(8,128)(2,1)S(1)} %collective-permute-done.1) | copy-start | bytes 786436
  16.8 9.3 %collective-permute-start.2 = (bf16[4,1,128,256]{2,3,1,0:T(8,128)(2,1)S(1)}, bf16[4,1,128,256]{2,3,1,0:T(8,128)(2,1)S(1)}, u32[]{:S(2)}, u32[]{:S(2)}) collective-permute-start(bf16[4,1,128,256]{2,3,1,0:T(8,128)(2,1)S(1)} %get-tuple-element.68), channel_id=1, source_target_pairs={{0,1},{1,2},{2,3},{3,0},{4,5},{5,6},{6,7},{7,4},{8,9},{9,10},{10,1... | collective-permute-start | bytes 786440 | tf_op jit(solution)/shard_map/ppermute | solution.py:17
  18.4 7.7 collective-permute-start.3
  22.4 11.0 %copy-start.71 = (f32[1,256]{1,0:T(1,128)}, f32[1,256]{1,0:T(1,128)S(1)}, u32[]{:S(2)}) copy-start(f32[1,256]{1,0:T(1,128)S(1)} %get-tuple-element.75) | copy-start | bytes 3076
  22.4 11.0 %copy-start.73 = (f32[1,256]{1,0:T(1,128)}, f32[1,256]{1,0:T(1,128)S(1)}, u32[]{:S(2)}) copy-start(f32[1,256]{1,0:T(1,128)S(1)} %get-tuple-element.76) | copy-start | bytes 3076
  22.5 11.0 %copy-start.75 = (f32[1,256]{1,0:T(1,128)}, f32[1,256]{1,0:T(1,128)S(1)}, u32[]{:S(2)}) copy-start(f32[1,256]{1,0:T(1,128)S(1)} %get-tuple-element.77) | copy-start | bytes 3076
  22.5 11.0 %copy-start.77 = (f32[1,256]{1,0:T(1,128)}, f32[1,256]{1,0:T(1,128)S(1)}, u32[]{:S(2)}) copy-start(f32[1,256]{1,0:T(1,128)S(1)} %get-tuple-element.78) | copy-start | bytes 3076
  22.5 11.0 %copy-start.79 = (f32[1,256]{1,0:T(1,128)}, f32[1,256]{1,0:T(1,128)S(1)}, u32[]{:S(2)}) copy-start(f32[1,256]{1,0:T(1,128)S(1)} %get-tuple-element.79) | copy-start | bytes 3076
  22.5 11.0 %copy-start.81 = (f32[1,256]{1,0:T(1,128)}, f32[1,256]{1,0:T(1,128)S(1)}, u32[]{:S(2)}) copy-start(f32[1,256]{1,0:T(1,128)S(1)} %get-tuple-element.80) | copy-start | bytes 3076
  22.5 11.0 %copy-start.83 = (f32[1,256]{1,0:T(1,128)}, f32[1,256]{1,0:T(1,128)S(1)}, u32[]{:S(2)}) copy-start(f32[1,256]{1,0:T(1,128)S(1)} %get-tuple-element.81) | copy-start | bytes 3076
  22.5 11.0 %copy-start.85 = (f32[1,256]{1,0:T(1,128)}, f32[1,256]{1,0:T(1,128)S(1)}, u32[]{:S(2)}) copy-start(f32[1,256]{1,0:T(1,128)S(1)} %get-tuple-element.82) | copy-start | bytes 3076
  22.5 11.0 %copy-start.87 = (f32[1,256]{1,0:T(1,128)}, f32[1,256]{1,0:T(1,128)S(1)}, u32[]{:S(2)}) copy-start(f32[1,256]{1,0:T(1,128)S(1)} %get-tuple-element.83) | copy-start | bytes 3076
  22.5 11.0 %copy-start.89 = (f32[1,256]{1,0:T(1,128)}, f32[1,256]{1,0:T(1,128)S(1)}, u32[]{:S(2)}) copy-start(f32[1,256]{1,0:T(1,128)S(1)} %get-tuple-element.84) | copy-start | bytes 3076
  22.5 11.0 %copy-start.91 = (f32[1,256]{1,0:T(1,128)}, f32[1,256]{1,0:T(1,128)S(1)}, u32[]{:S(2)}) copy-start(f32[1,256]{1,0:T(1,128)S(1)} %get-tuple-element.85) | copy-start | bytes 3076
  22.6 11.0 %copy-start.93 = (f32[1,256]{1,0:T(1,128)}, f32[1,256]{1,0:T(1,128)S(1)}, u32[]{:S(2)}) copy-start(f32[1,256]{1,0:T(1,128)S(1)} %get-tuple-element.86) | copy-start | bytes 3076
  22.6 11.0 %copy-start.95 = (f32[1,256]{1,0:T(1,128)}, f32[1,256]{1,0:T(1,128)S(1)}, u32[]{:S(2)}) copy-start(f32[1,256]{1,0:T(1,128)S(1)} %get-tuple-element.87) | copy-start | bytes 3076
  22.6 11.0 %copy-start.97 = (f32[1,256]{1,0:T(1,128)}, f32[1,256]{1,0:T(1,128)S(1)}, u32[]{:S(2)}) copy-start(f32[1,256]{1,0:T(1,128)S(1)} %get-tuple-element.88) | copy-start | bytes 3076
  22.6 11.0 %copy-start.99 = (f32[1,256]{1,0:T(1,128)}, f32[1,256]{1,0:T(1,128)S(1)}, u32[]{:S(2)}) copy-start(f32[1,256]{1,0:T(1,128)S(1)} %get-tuple-element.89) | copy-start | bytes 3076
  22.6 11.0 %copy-start.101 = (f32[1,256]{1,0:T(1,128)}, f32[1,256]{1,0:T(1,128)S(1)}, u32[]{:S(2)}) copy-start(f32[1,256]{1,0:T(1,128)S(1)} %get-tuple-element.90) | copy-start | bytes 3076
  22.6 11.0 %copy-start.103 = (f32[1,256]{1,0:T(1,128)}, f32[1,256]{1,0:T(1,128)S(1)}, u32[]{:S(2)}) copy-start(f32[1,256]{1,0:T(1,128)S(1)} %get-tuple-element.91) | copy-start | bytes 3076
  22.6 11.0 %copy-start.105 = (f32[1,256]{1,0:T(1,128)}, f32[1,256]{1,0:T(1,128)S(1)}, u32[]{:S(2)}) copy-start(f32[1,256]{1,0:T(1,128)S(1)} %get-tuple-element.92) | copy-start | bytes 3076
  22.6 11.0 %copy-start.107 = (f32[1,256]{1,0:T(1,128)}, f32[1,256]{1,0:T(1,128)S(1)}, u32[]{:S(2)}) copy-start(f32[1,256]{1,0:T(1,128)S(1)} %get-tuple-element.93) | copy-start | bytes 3076
  27.4 6.2 copy-start.8
  27.4 6.2 copy-start.10
  122.3 501.2 %all-reduce.7.cloned.1.call-start = ((), (), s32[]{:S(2)}) async-start(), calls=%async_computation.1 | async-start | bytes 524288 | tf_op jit(solution)/shard_map/psum | solution.py:109
  359.7 9.5 %copy-start.18 = (bf16[2,4,128,256]{2,3,1,0:T(8,128)(2,1)S(1)}, bf16[2,4,128,256]{2,3,1,0:T(8,128)(2,1)}, u32[]{:S(2)}) copy-start(bf16[2,4,128,256]{2,3,1,0:T(8,128)(2,1)} %copy-done.17) | copy-start | bytes 1572868
  361.4 9.8 %copy-start.53 = (f32[4]{0:T(128)}, f32[4]{0:T(128)S(1)}, u32[]{:S(2)}) copy-start(f32[4]{0:T(128)S(1)} %select_reduce_fusion) | copy-start | bytes 52
  362.0 11.6 %copy-start.112 = (f32[4]{0:T(128)}, f32[4]{0:T(128)S(1)}, u32[]{:S(2)}) copy-start(f32[4]{0:T(128)S(1)} %get-tuple-element.104) | copy-start | bytes 52
  375.7 247.8 %copy-start.113 = (f32[4]{0:T(128)S(1)}, f32[4]{0:T(128)}, u32[]{:S(2)}) copy-start(f32[4]{0:T(128)} %copy-done.112) | copy-start | bytes 52
  623.5 7.1 copy-start.22
  623.5 7.5 copy-start.35
  623.5 8.1 %copy-start.41 = (f32[4,64,64]{2,1,0:T(8,128)S(1)}, f32[4,64,64]{2,1,0:T(8,128)}, u32[]{:S(2)}) copy-start(f32[4,64,64]{2,1,0:T(8,128)} %copy-done.40) | copy-start | bytes 196612
  623.5 8.9 %copy-start.20 = (f32[4,64,64]{2,1,0:T(8,128)S(1)}, f32[4,64,64]{2,1,0:T(8,128)}, u32[]{:S(2)}) copy-start(f32[4,64,64]{2,1,0:T(8,128)} %copy-done.19) | copy-start | bytes 196612
  623.5 9.3 %copy-start.33 = (f32[4,64,64]{2,1,0:T(8,128)S(1)}, f32[4,64,64]{2,1,0:T(8,128)}, u32[]{:S(2)}) copy-start(f32[4,64,64]{2,1,0:T(8,128)} %copy-done.32) | copy-start | bytes 196612
  625.1 8.4 %copy-start.39 = (f32[4,64,64]{2,1,0:T(8,128)S(1)}, f32[4,64,64]{2,1,0:T(8,128)}, u32[]{:S(2)}) copy-start(f32[4,64,64]{2,1,0:T(8,128)} %copy-done.38) | copy-start | bytes 196612
  627.7 7.1 copy-start.31
  633.5 12.1 %copy-start.109 = (f32[4]{0:T(128)S(1)}, f32[4]{0:T(128)}, u32[]{:S(2)}) copy-start(f32[4]{0:T(128)} %get-tuple-element.102) | copy-start | bytes 52
  633.5 12.1 %copy-start.110 = (f32[4]{0:T(128)S(1)}, f32[4]{0:T(128)}, u32[]{:S(2)}) copy-start(f32[4]{0:T(128)} %get-tuple-element.103) | copy-start | bytes 52
  633.9 14.2 %copy-start.54 = (f32[4]{0:T(128)S(1)}, f32[4]{0:T(128)}, u32[]{:S(2)}) copy-start(f32[4]{0:T(128)} %copy-done.53) | copy-start | bytes 52
  633.9 14.3 %copy-start.50 = (pred[64,64]{1,0:T(8,128)(4,1)S(1)}, pred[64,64]{1,0:T(8,128)(4,1)}, u32[]{:S(2)}) copy-start(pred[64,64]{1,0:T(8,128)(4,1)} %iota_compare_fusion) | copy-start | bytes 12292
  634.0 14.2 %copy-start.51 = (f32[2,4,128]{2,1,0:T(4,128)S(1)}, f32[2,4,128]{2,1,0:T(4,128)}, u32[]{:S(2)}) copy-start(f32[2,4,128]{2,1,0:T(4,128)} %broadcast_divide_fusion.7) | copy-start | bytes 12292
  642.9 13.3 %copy-start.13 = (bf16[1,4,128,256]{2,3,1,0:T(8,128)(2,1)S(1)}, bf16[1,4,128,256]{2,3,1,0:T(8,128)(2,1)}, u32[]{:S(2)}) copy-start(bf16[1,4,128,256]{2,3,1,0:T(8,128)(2,1)} %copy-done.12) | copy-start | bytes 786436
  645.6 10.6 %copy-start.2 = (bf16[4,6,129,256]{2,3,1,0:T(8,128)(2,1)S(1)}, bf16[4,6,129,256]{2,3,1,0:T(8,128)(2,1)}, u32[]{:S(2)}) copy-start(bf16[4,6,129,256]{2,3,1,0:T(8,128)(2,1)} %copy-done.1) | copy-start | bytes 4755460
  645.6 10.6 %copy-start.7 = (bf16[2,4,128,256]{2,3,1,0:T(8,128)(2,1)S(1)}, bf16[2,4,128,256]{2,3,1,0:T(8,128)(2,1)}, u32[]{:S(2)}) copy-start(bf16[2,4,128,256]{2,3,1,0:T(8,128)(2,1)} %copy-done.5) | copy-start | bytes 1572868
  645.6 10.6 %copy-start.11 = (bf16[4,5,128,256]{2,3,1,0:T(8,128)(2,1)S(1)}, bf16[4,5,128,256]{2,3,1,0:T(8,128)(2,1)}, u32[]{:S(2)}) copy-start(bf16[4,5,128,256]{2,3,1,0:T(8,128)(2,1)} %copy-done.10) | copy-start | bytes 3932164
  645.6 10.6 %copy-start.16 = (bf16[1,4,128,256]{2,3,1,0:T(8,128)(2,1)S(1)}, bf16[1,4,128,256]{2,3,1,0:T(8,128)(2,1)}, u32[]{:S(2)}) copy-start(bf16[1,4,128,256]{2,3,1,0:T(8,128)(2,1)} %copy-done.14) | copy-start | bytes 786436
  651.2 9.8 %copy-start.3 = (bf16[2,4,128,4,64]{2,4,3,1,0:T(8,128)(2,1)}, bf16[2,4,128,4,64]{2,4,3,1,0:T(8,128)(2,1)S(1)}, u32[]{:S(2)}) copy-start(bf16[2,4,128,4,64]{2,4,3,1,0:T(8,128)(2,1)S(1)} %copy.74) | copy-start | bytes 1572868
  652.1 88.6 %collective-permute-start.4 = (bf16[1,4,128,256]{2,3,1,0:T(8,128)(2,1)}, bf16[1,4,128,256]{2,3,1,0:T(8,128)(2,1)}, u32[]{:S(2)}, u32[]{:S(2)}) collective-permute-start(bf16[1,4,128,256]{2,3,1,0:T(8,128)(2,1)} %get-tuple-element.71), channel_id=1, source_target_pairs={{0,4},{4,8},{8,12},{12,16},{16,20},{20,24},{24,28},{28,32},{32,36}... | collective-permute-start | bytes 786440 | tf_op jit(solution)/shard_map/ppermute | solution.py:17
  652.8 8.2 %copy-start.9 = (bf16[4,5,128,256]{2,3,1,0:T(8,128)(2,1)S(1)}, bf16[4,5,128,256]{2,3,1,0:T(8,128)(2,1)}, u32[]{:S(2)}) copy-start(bf16[4,5,128,256]{2,3,1,0:T(8,128)(2,1)} %copy-done.8) | copy-start | bytes 3932164
  652.8 87.9 %collective-permute-start.5 = (bf16[1,4,128,256]{2,3,1,0:T(8,128)(2,1)}, bf16[1,4,128,256]{2,3,1,0:T(8,128)(2,1)}, u32[]{:S(2)}, u32[]{:S(2)}) collective-permute-start(bf16[1,4,128,256]{2,3,1,0:T(8,128)(2,1)} %get-tuple-element.72), channel_id=1, source_target_pairs={{4,0},{8,4},{12,8},{16,12},{20,16},{24,20},{28,24},{32,28},{36,32}... | collective-permute-start | bytes 786440 | tf_op jit(solution)/shard_map/ppermute | solution.py:20
  662.5 88.2 %copy-start.4 = (bf16[2,4,128,4,64]{2,4,3,1,0:T(8,128)(2,1)S(1)}, bf16[2,4,128,4,64]{2,4,3,1,0:T(8,128)(2,1)}, u32[]{:S(2)}) copy-start(bf16[2,4,128,4,64]{2,4,3,1,0:T(8,128)(2,1)} %copy-done.3) | copy-start | bytes 1572868
  741.8 8.8 %collective-permute-start.6 = (bf16[4,1,128,256]{2,3,1,0:T(8,128)(2,1)S(1)}, bf16[4,1,128,256]{2,3,1,0:T(8,128)(2,1)S(1)}, u32[]{:S(2)}, u32[]{:S(2)}) collective-permute-start(bf16[4,1,128,256]{2,3,1,0:T(8,128)(2,1)S(1)} %get-tuple-element.64), channel_id=1, source_target_pairs={{0,1},{1,2},{2,3},{3,0},{4,5},{5,6},{6,7},{7,4},{8,9},{9,10},{10,1... | collective-permute-start | bytes 786440 | tf_op jit(solution)/shard_map/ppermute | solution.py:17
  741.9 8.7 %collective-permute-start.7 = (bf16[4,1,128,256]{2,3,1,0:T(8,128)(2,1)S(1)}, bf16[4,1,128,256]{2,3,1,0:T(8,128)(2,1)S(1)}, u32[]{:S(2)}, u32[]{:S(2)}) collective-permute-start(bf16[4,1,128,256]{2,3,1,0:T(8,128)(2,1)S(1)} %get-tuple-element.65), channel_id=1, source_target_pairs={{1,0},{2,1},{3,2},{0,3},{5,4},{6,5},{7,6},{4,7},{9,8},{10,9},{11,1... | collective-permute-start | bytes 786440 | tf_op jit(solution)/shard_map/ppermute | solution.py:20
  (61 other events, 237.0 us)
Sparse Core Ops, SparseCore 0:
  122.5 237.1 all-reduce.4
  376.8 246.6 all-reduce.6
where the time goes:
time: 783 us; the launch traced here: 775 us
  waiting for transfers between devices  410 us (52%)
  blocking collectives  233 us (30%)
  other arithmetic  44.9 us (6%)
  matrix products  36.3 us (5%)
  local copies, waits for them, and re-layouts  19.2 us (2%)
  between operations  16.2 us (2%)
  starting transfers between devices  15.1 us (2%)
    psum x1, waiting for transfers between devices, per_device(): sigma = lax.psum(cov_part, ('gx', 'gy')) / count + EPS * eye  236 us
    psum x1, waiting for transfers between devices, per_device(): dwhite, dsum = lax.psum((dwhite_part, dsum_part), ('gx', 'gy'))  168 us
    psum x1, blocking collectives, per_device(): count, total = lax.psum((count_part, sum_part), ('gx', 'gy'))  79.1 us
    psum x1, blocking collectives, per_device(): ker_sum, mix_sum = lax.psum((ker_part, mix_part), ('gx', 'gy'))  78.1 us
    psum x1, blocking collectives, per_device(): dwhite, dsum = lax.psum((dwhite_part, dsum_part), ('gx', 'gy'))  76.3 us
  transfers between devices with their start and end apart: 10, of which 5 were waited for; matrix products, arithmetic and copies ran while one was open for 3% of the time, Pallas kernels for 0%

commit v1 on v0

--- a/solution.py
+++ b/solution.py
@@ -84,7 +84,12 @@
     cov_part = jnp.einsum(
         "abzgi,abzgj->gij", keep_own[..., None, None] * cent_own, cent_own, precision=HI
     )
-    sigma = lax.psum(cov_part, ("gx", "gy")) / count + EPS * eye
+
+    def do_the_ranges(in_array):
+        kept_arr = jnp.sum(jax.lax.all_gather(in_array, axis_name=("gx", "gy")), axis=0)
+        return kept_arr
+
+    sigma = do_the_ranges(cov_part) / count + EPS * eye
     white = jax.vmap(whiten)(sigma)
     centered = field.reshape(ext_x, ext_y, depth, groups, width) - mean
     gain = norm_gain.reshape(groups, width)

time: 783 us -> 707 us (0.903)
  waiting for transfers between devices: 410 us -> 320 us
    psum x1 -> x0, waiting for transfers between devices: 236 us -> none  [per_device(): sigma = lax.psum(cov_part, ('gx', 'gy')) / count + EPS * eye]
    all_gather x0 -> x1, waiting for transfers between devices: none -> 142 us  [do_the_ranges(): jax.lax.all_gather(in_array, axis_name=('gx', 'gy'))]
    reduce_sum x1 -> x2, other arithmetic: 2.54 us -> 12.5 us  [the longest x1 12.3 us: do_the_ranges(): jnp.sum(jax.lax.all_gather(in_array, axis_name=('gx', 'gy')), axis=0)]
where the time goes in v1:
time: 707 us; the launch traced here: 699 us
  waiting for transfers between devices  320 us (45%)
  blocking collectives  234 us (33%)
  other arithmetic  52.6 us (7%)
  matrix products  41.9 us (6%)
  local copies, waits for them, and re-layouts  19 us (3%)
  between operations  16.2 us (2%)
  starting transfers between devices  15.1 us (2%)
    psum x1, waiting for transfers between devices, per_device(): dwhite, dsum = lax.psum((dwhite_part, dsum_part), ('gx', 'gy'))  169 us
    all_gather x1, waiting for transfers between devices, do_the_ranges(): jax.lax.all_gather(in_array, axis_name=('gx', 'gy'))  142 us
    psum x1, blocking collectives, per_device(): count, total = lax.psum((count_part, sum_part), ('gx', 'gy'))  79.1 us
    psum x1, blocking collectives, per_device(): ker_sum, mix_sum = lax.psum((ker_part, mix_part), ('gx', 'gy'))  78.1 us
    psum x1, blocking collectives, per_device(): dwhite, dsum = lax.psum((dwhite_part, dsum_part), ('gx', 'gy'))  76.9 us
  transfers between devices with their start and end apart: 10, of which 5 were waited for; matrix products, arithmetic and copies ran while one was open for 3% of the time, Pallas kernels for 0%

profile of v1, /device:TPU:32, one launch (start us, length us, event | category | flops | bytes accessed | tf_op | source)
XLA Modules:
  0.0 698.7 jit_solution(6259132379625540567)
XLA Ops:
  7.3 1.3 copy.86
  8.7 3.8 collective-permute-start.1
  12.6 0.7 subtract_convert_fusion
  13.2 0.9 fusion.156
  14.2 2.4 collective-permute-done
  16.7 1.7 collective-permute-start.2
  18.3 1.7 collective-permute-start.3
  20.8 5.2 collective-permute-done.2
  26.3 0.7 fusion.152
  27.3 5.1 maximum_maximum_fusion
  32.7 4.6 fusion.47
  37.3 0.8 copy-done.22
  38.3 79.1 %all-reduce = (f32[256]{0:T(256)S(1)}, f32[]{:T(128)}) all-reduce(f32[256]{0:T(256)S(1)} %multiply_reduce_fusion, f32[]{:T(128)} %fusion.150), channel_id=1, replica_groups=mesh['gx'=64,'gy'=4] {'gx','gy'}, use_global_device_ids=true, to_apply=%region_1.0 | all-reduce | flops 257 | bytes 2056 | tf_op jit(solution)/shard_map/psum | solution.py:81
  117.4 0.7 broadcast_divide_fusion.8
  118.1 3.2 fusion.10
  122.1 0.7 mul.785
  122.8 2.1 copy.103
  125.4 1.3 broadcast_divide_fusion.7
  126.7 142.1 %all-gather.3.cloned.1.call-done = f32[1024,64,64]{2,1,0:T(8,128)} async-done(((f32[4,64,64]{2,1,0:T(8,128)}), f32[1024,64,64]{2,1,0:T(8,128)}) %all-gather.3.cloned.1.call-update) | async-done | bytes 16777232 | tf_op jit(solution)/shard_map/all_gather | solution.py:89
  268.8 12.3 %reduce_sum.314 = f32[4,64,64]{2,1,0:T(8,128)S(1)} reduce(f32[256,4,64,64]{3,2,1,0:T(8,128)} %bitcast.241, f32[]{:T(128)} %constant.12.clone.1), dimensions={0}, to_apply=%region_4.0 | reduce | flops 4177920 | bytes 16842756 | tf_op jit(solution)/shard_map/reduce_sum | solution.py:89
  281.2 0.9 select_reduce_fusion
  282.1 0.8 broadcast_divide_fusion.2
  289.4 1.3 multiply_convert_fusion
  291.3 1.9 convolution_bitcast_fusion.6
  293.1 2.1 fusion.157
  295.2 0.9 convolution_bitcast_fusion.3
  296.2 1.4 convolution_bitcast_fusion.1
  297.6 1.1 copy.102
  298.7 76.9 %psum.45 = f32[4,64]{1,0:T(4,128)S(1)} all-reduce(f32[4,64]{1,0:T(4,128)S(1)} %get-tuple-element.109), channel_id=1, replica_groups=mesh['gx'=64,'gy'=4] {'gx','gy'}, use_global_device_ids=true, to_apply=%region_10.11 | all-reduce | flops 256 | bytes 2048 | tf_op jit(solution)/shard_map/psum | solution.py:114
  375.6 168.7 %all-reduce.4.cloned.1.call-done = (f32[4,64,64]{2,1,0:T(8,128)}, f32[4,64,64]{2,1,0:T(8,128)}) async-done(((f32[4,64,64]{2,1,0:T(8,128)}, f32[4,64,64]{2,1,0:T(8,128)}), (f32[4,64,64]{2,1,0:T(8,128)}, f32[4,64,64]{2,1,0:T(8,128)})) %all-reduce.4.cloned.1.call-update) | async-done | bytes 131088 | tf_op jit(solution)/shard_map/psum | solution.py:114
  544.3 1.5 convolution_add_fusion.14
  545.8 1.5 fusion.114
  547.2 1.2 fusion.166
  548.4 1.3 convolution_add_fusion.13
  550.2 1.3 convolution_add_fusion.10
  551.5 1.3 fusion.113
  552.8 1.2 fusion.168
  553.9 1.3 convolution_add_fusion.9
  555.7 1.3 convolution_add_fusion.6
  556.9 1.3 fusion.112
  558.2 1.2 fusion.169
  563.0 0.8 convolution_bitcast_fusion.4
  564.7 1.1 convolution_add_fusion.3
  565.7 1.7 copy.130
  567.5 2.6 multiply_reduce_fusion.1
  570.0 1.6 copy.131
  571.7 3.0 fusion.9
  574.8 0.9 fusion.153
  575.7 0.7 collective-permute-start.4
  576.4 3.4 collective-permute-start.5
  579.8 5.1 fusion.90
  584.9 1.5 fusion.89
  586.5 78.1 %psum.46 = f32[27,256]{1,0:T(8,128)S(1)} all-reduce(f32[27,256]{1,0:T(8,128)S(1)} %stack.111), channel_id=1, replica_groups=mesh['gx'=64,'gy'=4] {'gx','gy'}, use_global_device_ids=true, to_apply=%region_38.39 | all-reduce | flops 6912 | bytes 55296 | tf_op jit(solution)/shard_map/psum | solution.py:141
  664.6 1.1 pad_maximum_fusion.12
  665.8 3.2 collective-permute-start.7
  669.7 2.0 copy.136
  671.7 1.6 broadcast_multiply_fusion
  673.3 1.3 collective-permute-done.6
  674.5 1.4 pad_maximum_fusion.3
  675.9 0.7 fusion.151
  676.6 1.6 pad_maximum_fusion.5
  678.5 4.6 pad_maximum_fusion.1
  683.3 6.3 fusion.93
  689.6 2.0 copy.137
  (278 shorter events, 16.1 us)
Async XLA Ops:
  7.2 283.6 %copy-start = (bf16[4,64,64]{2,1,0:T(8,128)(2,1)S(1)}, bf16[4,64,64]{2,1,0:T(8,128)(2,1)}, u32[]{:S(2)}) copy-start(bf16[4,64,64]{2,1,0:T(8,128)(2,1)} %param.9) | copy-start | bytes 98308
  7.2 12.8 %copy-start.45 = (s32[2,4,128]{2,1,0:T(4,128)S(1)}, s32[2,4,128]{2,1,0:T(4,128)}, u32[]{:S(2)}) copy-start(s32[2,4,128]{2,1,0:T(4,128)} %param.7) | copy-start | bytes 12292
  7.2 13.4 %copy-start.44 = (bf16[27,256]{1,0:T(8,128)(2,1)S(1)}, bf16[27,256]{1,0:T(8,128)(2,1)}, u32[]{:S(2)}) copy-start(bf16[27,256]{1,0:T(8,128)(2,1)} %param.8) | copy-start | bytes 41476
  7.2 261.6 %all-gather.3.cloned.1.call-start = ((), (), s32[]{:S(2)}) async-start(), calls=%async_computation | async-start | bytes 33685504 | tf_op jit(solution)/shard_map/all_gather | solution.py:89
  8.6 18.4 %copy-start.6 = (bf16[2,4,128,256]{2,3,1,0:T(8,128)(2,1)}, bf16[2,4,128,256]{2,3,1,0:T(8,128)(2,1)S(1)}, u32[]{:S(2)}) copy-start(bf16[2,4,128,256]{2,3,1,0:T(8,128)(2,1)S(1)} %copy.86) | copy-start | bytes 1572868
  8.6 8.0 %collective-permute-start = (bf16[1,4,128,256]{2,3,1,0:T(8,128)(2,1)S(1)}, bf16[1,4,128,256]{2,3,1,0:T(8,128)(2,1)S(1)}, u32[]{:S(2)}, u32[]{:S(2)}) collective-permute-start(bf16[1,4,128,256]{2,3,1,0:T(8,128)(2,1)S(1)} %get-tuple-element.78), channel_id=1, source_target_pairs={{0,4},{4,8},{8,12},{12,16},{16,20},{20,24},{24,28},{28,32},{32,36}... | collective-permute-start | bytes 786440 | tf_op jit(solution)/shard_map/ppermute | solution.py:17
  8.7 7.9 %collective-permute-start.1 = (bf16[1,4,128,256]{2,3,1,0:T(8,128)(2,1)S(1)}, bf16[1,4,128,256]{2,3,1,0:T(8,128)(2,1)S(1)}, u32[]{:S(2)}, u32[]{:S(2)}) collective-permute-start(bf16[1,4,128,256]{2,3,1,0:T(8,128)(2,1)S(1)} %get-tuple-element.77), channel_id=1, source_target_pairs={{4,0},{8,4},{12,8},{16,12},{20,16},{24,20},{28,24},{32,28},{36,32}... | collective-permute-start | bytes 786440 | tf_op jit(solution)/shard_map/ppermute | solution.py:20
  14.1 18.2 %copy-start.46 = (f32[1,256]{1,0:T(1,128)}, f32[1,256]{1,0:T(1,128)S(1)}, u32[]{:S(2)}) copy-start(f32[1,256]{1,0:T(1,128)S(1)} %get-tuple-element.100) | copy-start | bytes 3076
  14.1 18.2 %copy-start.48 = (f32[1,256]{1,0:T(1,128)}, f32[1,256]{1,0:T(1,128)S(1)}, u32[]{:S(2)}) copy-start(f32[1,256]{1,0:T(1,128)S(1)} %get-tuple-element.101) | copy-start | bytes 3076
  14.2 18.2 %copy-start.50 = (f32[1,256]{1,0:T(1,128)}, f32[1,256]{1,0:T(1,128)S(1)}, u32[]{:S(2)}) copy-start(f32[1,256]{1,0:T(1,128)S(1)} %get-tuple-element.102) | copy-start | bytes 3076
  14.2 18.2 %copy-start.52 = (f32[1,256]{1,0:T(1,128)}, f32[1,256]{1,0:T(1,128)S(1)}, u32[]{:S(2)}) copy-start(f32[1,256]{1,0:T(1,128)S(1)} %get-tuple-element.103) | copy-start | bytes 3076
  14.2 18.2 %copy-start.54 = (f32[1,256]{1,0:T(1,128)}, f32[1,256]{1,0:T(1,128)S(1)}, u32[]{:S(2)}) copy-start(f32[1,256]{1,0:T(1,128)S(1)} %get-tuple-element.104) | copy-start | bytes 3076
  14.2 18.2 %copy-start.56 = (f32[1,256]{1,0:T(1,128)}, f32[1,256]{1,0:T(1,128)S(1)}, u32[]{:S(2)}) copy-start(f32[1,256]{1,0:T(1,128)S(1)} %get-tuple-element.105) | copy-start | bytes 3076
  16.6 15.8 %copy-start.12 = (bf16[1,4,128,256]{2,3,1,0:T(8,128)(2,1)}, bf16[1,4,128,256]{2,3,1,0:T(8,128)(2,1)S(1)}, u32[]{:S(2)}) copy-start(bf16[1,4,128,256]{2,3,1,0:T(8,128)(2,1)S(1)} %collective-permute-done) | copy-start | bytes 786436
  16.6 15.8 %copy-start.14 = (bf16[1,4,128,256]{2,3,1,0:T(8,128)(2,1)}, bf16[1,4,128,256]{2,3,1,0:T(8,128)(2,1)S(1)}, u32[]{:S(2)}) copy-start(bf16[1,4,128,256]{2,3,1,0:T(8,128)(2,1)S(1)} %collective-permute-done.1) | copy-start | bytes 786436
  16.7 9.3 %collective-permute-start.2 = (bf16[4,1,128,256]{2,3,1,0:T(8,128)(2,1)S(1)}, bf16[4,1,128,256]{2,3,1,0:T(8,128)(2,1)S(1)}, u32[]{:S(2)}, u32[]{:S(2)}) collective-permute-start(bf16[4,1,128,256]{2,3,1,0:T(8,128)(2,1)S(1)} %get-tuple-element.72), channel_id=1, source_target_pairs={{0,1},{1,2},{2,3},{3,0},{4,5},{5,6},{6,7},{7,4},{8,9},{9,10},{10,1... | collective-permute-start | bytes 786440 | tf_op jit(solution)/shard_map/ppermute | solution.py:17
  18.3 7.7 %collective-permute-start.3 = (bf16[4,1,128,256]{2,3,1,0:T(8,128)(2,1)S(1)}, bf16[4,1,128,256]{2,3,1,0:T(8,128)(2,1)S(1)}, u32[]{:S(2)}, u32[]{:S(2)}) collective-permute-start(bf16[4,1,128,256]{2,3,1,0:T(8,128)(2,1)S(1)} %get-tuple-element.73), channel_id=1, source_target_pairs={{1,0},{2,1},{3,2},{0,3},{5,4},{6,5},{7,6},{4,7},{9,8},{10,9},{11,1... | collective-permute-start | bytes 786440 | tf_op jit(solution)/shard_map/ppermute | solution.py:20
  20.6 11.8 %copy-start.58 = (f32[1,256]{1,0:T(1,128)}, f32[1,256]{1,0:T(1,128)S(1)}, u32[]{:S(2)}) copy-start(f32[1,256]{1,0:T(1,128)S(1)} %get-tuple-element.79) | copy-start | bytes 3076
  20.6 11.8 %copy-start.60 = (f32[1,256]{1,0:T(1,128)}, f32[1,256]{1,0:T(1,128)S(1)}, u32[]{:S(2)}) copy-start(f32[1,256]{1,0:T(1,128)S(1)} %get-tuple-element.80) | copy-start | bytes 3076
  20.6 11.8 %copy-start.62 = (f32[1,256]{1,0:T(1,128)}, f32[1,256]{1,0:T(1,128)S(1)}, u32[]{:S(2)}) copy-start(f32[1,256]{1,0:T(1,128)S(1)} %get-tuple-element.81) | copy-start | bytes 3076
  20.7 11.8 %copy-start.64 = (f32[1,256]{1,0:T(1,128)}, f32[1,256]{1,0:T(1,128)S(1)}, u32[]{:S(2)}) copy-start(f32[1,256]{1,0:T(1,128)S(1)} %get-tuple-element.82) | copy-start | bytes 3076
  20.7 11.8 %copy-start.66 = (f32[1,256]{1,0:T(1,128)}, f32[1,256]{1,0:T(1,128)S(1)}, u32[]{:S(2)}) copy-start(f32[1,256]{1,0:T(1,128)S(1)} %get-tuple-element.83) | copy-start | bytes 3076
  20.7 11.8 %copy-start.68 = (f32[1,256]{1,0:T(1,128)}, f32[1,256]{1,0:T(1,128)S(1)}, u32[]{:S(2)}) copy-start(f32[1,256]{1,0:T(1,128)S(1)} %get-tuple-element.84) | copy-start | bytes 3076
  20.7 11.8 %copy-start.70 = (f32[1,256]{1,0:T(1,128)}, f32[1,256]{1,0:T(1,128)S(1)}, u32[]{:S(2)}) copy-start(f32[1,256]{1,0:T(1,128)S(1)} %get-tuple-element.85) | copy-start | bytes 3076
  20.7 11.8 %copy-start.72 = (f32[1,256]{1,0:T(1,128)}, f32[1,256]{1,0:T(1,128)S(1)}, u32[]{:S(2)}) copy-start(f32[1,256]{1,0:T(1,128)S(1)} %get-tuple-element.86) | copy-start | bytes 3076
  20.7 11.8 %copy-start.74 = (f32[1,256]{1,0:T(1,128)}, f32[1,256]{1,0:T(1,128)S(1)}, u32[]{:S(2)}) copy-start(f32[1,256]{1,0:T(1,128)S(1)} %get-tuple-element.87) | copy-start | bytes 3076
  20.7 11.8 %copy-start.76 = (f32[1,256]{1,0:T(1,128)}, f32[1,256]{1,0:T(1,128)S(1)}, u32[]{:S(2)}) copy-start(f32[1,256]{1,0:T(1,128)S(1)} %get-tuple-element.88) | copy-start | bytes 3076
  20.7 11.8 %copy-start.78 = (f32[1,256]{1,0:T(1,128)}, f32[1,256]{1,0:T(1,128)S(1)}, u32[]{:S(2)}) copy-start(f32[1,256]{1,0:T(1,128)S(1)} %get-tuple-element.89) | copy-start | bytes 3076
  20.7 11.8 %copy-start.80 = (f32[1,256]{1,0:T(1,128)}, f32[1,256]{1,0:T(1,128)S(1)}, u32[]{:S(2)}) copy-start(f32[1,256]{1,0:T(1,128)S(1)} %get-tuple-element.90) | copy-start | bytes 3076
  20.7 11.8 %copy-start.82 = (f32[1,256]{1,0:T(1,128)}, f32[1,256]{1,0:T(1,128)S(1)}, u32[]{:S(2)}) copy-start(f32[1,256]{1,0:T(1,128)S(1)} %get-tuple-element.91) | copy-start | bytes 3076
  20.8 11.8 %copy-start.84 = (f32[1,256]{1,0:T(1,128)}, f32[1,256]{1,0:T(1,128)S(1)}, u32[]{:S(2)}) copy-start(f32[1,256]{1,0:T(1,128)S(1)} %get-tuple-element.92) | copy-start | bytes 3076
  20.8 11.8 %copy-start.86 = (f32[1,256]{1,0:T(1,128)}, f32[1,256]{1,0:T(1,128)S(1)}, u32[]{:S(2)}) copy-start(f32[1,256]{1,0:T(1,128)S(1)} %get-tuple-element.93) | copy-start | bytes 3076
  20.8 11.8 %copy-start.88 = (f32[1,256]{1,0:T(1,128)}, f32[1,256]{1,0:T(1,128)S(1)}, u32[]{:S(2)}) copy-start(f32[1,256]{1,0:T(1,128)S(1)} %get-tuple-element.94) | copy-start | bytes 3076
  20.8 11.8 %copy-start.90 = (f32[1,256]{1,0:T(1,128)}, f32[1,256]{1,0:T(1,128)S(1)}, u32[]{:S(2)}) copy-start(f32[1,256]{1,0:T(1,128)S(1)} %get-tuple-element.95) | copy-start | bytes 3076
  20.8 11.8 %copy-start.92 = (f32[1,256]{1,0:T(1,128)}, f32[1,256]{1,0:T(1,128)S(1)}, u32[]{:S(2)}) copy-start(f32[1,256]{1,0:T(1,128)S(1)} %get-tuple-element.96) | copy-start | bytes 3076
  20.8 11.8 %copy-start.94 = (f32[1,256]{1,0:T(1,128)}, f32[1,256]{1,0:T(1,128)S(1)}, u32[]{:S(2)}) copy-start(f32[1,256]{1,0:T(1,128)S(1)} %get-tuple-element.97) | copy-start | bytes 3076
  32.7 89.4 %copy-start.107 = (f32[256]{0:T(256)S(1)}, f32[256]{0:T(256)}, u32[]{:S(2)}) copy-start(f32[256]{0:T(256)} %param.10) | copy-start | bytes 3076
  121.3 422.9 %all-reduce.4.cloned.1.call-start = ((), (), s32[]{:S(2)}) async-start(), calls=%async_computation.1 | async-start | bytes 524288 | tf_op jit(solution)/shard_map/psum | solution.py:114
  281.2 8.2 %copy-start.23 = (bf16[2,4,128,256]{2,3,1,0:T(8,128)(2,1)S(1)}, bf16[2,4,128,256]{2,3,1,0:T(8,128)(2,1)}, u32[]{:S(2)}) copy-start(bf16[2,4,128,256]{2,3,1,0:T(8,128)(2,1)} %copy-done.22) | copy-start | bytes 1572868
  281.2 8.2 %copy-start.97 = (f32[4,64]{1,0:T(4,128)S(1)}, f32[4,64]{1,0:T(4,128)}, u32[]{:S(2)}) copy-start(f32[4,64]{1,0:T(4,128)} %copy-done.96) | copy-start | bytes 3076
  283.4 9.7 %copy-start.105 = (f32[4]{0:T(128)}, f32[4]{0:T(128)S(1)}, u32[]{:S(2)}) copy-start(f32[4]{0:T(128)S(1)} %get-tuple-element.108) | copy-start | bytes 52
  295.2 249.1 %copy-start.106 = (f32[4]{0:T(128)S(1)}, f32[4]{0:T(128)}, u32[]{:S(2)}) copy-start(f32[4]{0:T(128)} %copy-done.105) | copy-start | bytes 52
  544.3 15.1 %copy-start.37 = (f32[4,64,64]{2,1,0:T(8,128)S(1)}, f32[4,64,64]{2,1,0:T(8,128)}, u32[]{:S(2)}) copy-start(f32[4,64,64]{2,1,0:T(8,128)} %copy-done.36) | copy-start | bytes 196612
  545.7 14.5 %copy-start.29 = (f32[4,64,64]{2,1,0:T(8,128)S(1)}, f32[4,64,64]{2,1,0:T(8,128)}, u32[]{:S(2)}) copy-start(f32[4,64,64]{2,1,0:T(8,128)} %copy-done.28) | copy-start | bytes 196612
  548.4 12.6 %copy-start.21 = (f32[4,64,64]{2,1,0:T(8,128)S(1)}, f32[4,64,64]{2,1,0:T(8,128)}, u32[]{:S(2)}) copy-start(f32[4,64,64]{2,1,0:T(8,128)} %copy-done.20) | copy-start | bytes 196612
  549.7 11.7 %copy-start.33 = (f32[4,64,64]{2,1,0:T(8,128)S(1)}, f32[4,64,64]{2,1,0:T(8,128)}, u32[]{:S(2)}) copy-start(f32[4,64,64]{2,1,0:T(8,128)} %copy-done.32) | copy-start | bytes 196612
  549.8 11.7 %copy-start.43 = (f32[4,64,64]{2,1,0:T(8,128)S(1)}, f32[4,64,64]{2,1,0:T(8,128)}, u32[]{:S(2)}) copy-start(f32[4,64,64]{2,1,0:T(8,128)} %get-tuple-element.56) | copy-start | bytes 196612
  549.8 11.7 %copy-start.103 = (f32[4]{0:T(128)S(1)}, f32[4]{0:T(128)}, u32[]{:S(2)}) copy-start(f32[4]{0:T(128)} %get-tuple-element.106) | copy-start | bytes 52
  550.2 11.7 %copy-start.35 = (f32[4,64,64]{2,1,0:T(8,128)S(1)}, f32[4,64,64]{2,1,0:T(8,128)}, u32[]{:S(2)}) copy-start(f32[4,64,64]{2,1,0:T(8,128)} %copy-done.34) | copy-start | bytes 196612
  555.2 8.6 %copy-start.19 = (f32[4,64,64]{2,1,0:T(8,128)S(1)}, f32[4,64,64]{2,1,0:T(8,128)}, u32[]{:S(2)}) copy-start(f32[4,64,64]{2,1,0:T(8,128)} %copy-done.18) | copy-start | bytes 196612
  555.6 8.6 %copy-start.17 = (f32[4,64,64]{2,1,0:T(8,128)S(1)}, f32[4,64,64]{2,1,0:T(8,128)}, u32[]{:S(2)}) copy-start(f32[4,64,64]{2,1,0:T(8,128)} %copy-done.16) | copy-start | bytes 196612
  560.2 11.4 %copy-start.100 = (f32[4]{0:T(128)S(1)}, f32[4]{0:T(128)}, u32[]{:S(2)}) copy-start(f32[4]{0:T(128)} %copy-done.99) | copy-start | bytes 52
  560.2 11.4 %copy-start.98 = (f32[4,64]{1,0:T(4,128)S(1)}, f32[4,64]{1,0:T(4,128)}, u32[]{:S(2)}) copy-start(f32[4,64]{1,0:T(4,128)} %copy-done.96) | copy-start | bytes 3076
  560.3 11.4 %copy-start.101 = (pred[64,64]{0,1:T(8,128)(4,1)S(1)}, pred[64,64]{0,1:T(8,128)(4,1)}, u32[]{:S(2)}) copy-start(pred[64,64]{0,1:T(8,128)(4,1)} %iota_compare_fusion) | copy-start | bytes 12292
  560.3 11.4 %copy-start.102 = (f32[2,4,128]{2,1,0:T(4,128)S(1)}, f32[2,4,128]{2,1,0:T(4,128)}, u32[]{:S(2)}) copy-start(f32[2,4,128]{2,1,0:T(4,128)} %broadcast_divide_fusion.7) | copy-start | bytes 12292
  565.7 14.0 %copy-start.13 = (bf16[1,4,128,256]{2,3,1,0:T(8,128)(2,1)S(1)}, bf16[1,4,128,256]{2,3,1,0:T(8,128)(2,1)}, u32[]{:S(2)}) copy-start(bf16[1,4,128,256]{2,3,1,0:T(8,128)(2,1)} %copy-done.12) | copy-start | bytes 786436
  574.8 10.1 %copy-start.4 = (bf16[2,4,128,4,64]{2,4,3,1,0:T(8,128)(2,1)}, bf16[2,4,128,4,64]{2,4,3,1,0:T(8,128)(2,1)S(1)}, u32[]{:S(2)}) copy-start(bf16[2,4,128,4,64]{2,4,3,1,0:T(8,128)(2,1)S(1)} %copy.133) | copy-start | bytes 1572868
  575.7 88.9 %collective-permute-start.4 = (bf16[1,4,128,256]{2,3,1,0:T(8,128)(2,1)}, bf16[1,4,128,256]{2,3,1,0:T(8,128)(2,1)}, u32[]{:S(2)}, u32[]{:S(2)}) collective-permute-start(bf16[1,4,128,256]{2,3,1,0:T(8,128)(2,1)} %get-tuple-element.75), channel_id=1, source_target_pairs={{0,4},{4,8},{8,12},{12,16},{16,20},{20,24},{24,28},{28,32},{32,36}... | collective-permute-start | bytes 786440 | tf_op jit(solution)/shard_map/ppermute | solution.py:17
  576.4 8.5 %copy-start.10 = (bf16[4,5,128,256]{2,3,1,0:T(8,128)(2,1)S(1)}, bf16[4,5,128,256]{2,3,1,0:T(8,128)(2,1)}, u32[]{:S(2)}) copy-start(bf16[4,5,128,256]{2,3,1,0:T(8,128)(2,1)} %copy-done.9) | copy-start | bytes 3932164
  576.4 88.2 %collective-permute-start.5 = (bf16[1,4,128,256]{2,3,1,0:T(8,128)(2,1)}, bf16[1,4,128,256]{2,3,1,0:T(8,128)(2,1)}, u32[]{:S(2)}, u32[]{:S(2)}) collective-permute-start(bf16[1,4,128,256]{2,3,1,0:T(8,128)(2,1)} %get-tuple-element.76), channel_id=1, source_target_pairs={{4,0},{8,4},{12,8},{16,12},{20,16},{24,20},{28,24},{32,28},{36,32}... | collective-permute-start | bytes 786440 | tf_op jit(solution)/shard_map/ppermute | solution.py:20
  586.3 88.2 %copy-start.5 = (bf16[2,4,128,4,64]{2,4,3,1,0:T(8,128)(2,1)S(1)}, bf16[2,4,128,4,64]{2,4,3,1,0:T(8,128)(2,1)}, u32[]{:S(2)}) copy-start(bf16[2,4,128,4,64]{2,4,3,1,0:T(8,128)(2,1)} %copy-done.4) | copy-start | bytes 1572868
  665.7 8.8 %collective-permute-start.6 = (bf16[4,1,128,256]{2,3,1,0:T(8,128)(2,1)S(1)}, bf16[4,1,128,256]{2,3,1,0:T(8,128)(2,1)S(1)}, u32[]{:S(2)}, u32[]{:S(2)}) collective-permute-start(bf16[4,1,128,256]{2,3,1,0:T(8,128)(2,1)S(1)} %get-tuple-element.68), channel_id=1, source_target_pairs={{0,1},{1,2},{2,3},{3,0},{4,5},{5,6},{6,7},{7,4},{8,9},{9,10},{10,1... | collective-permute-start | bytes 786440 | tf_op jit(solution)/shard_map/ppermute | solution.py:17
  665.8 8.7 %collective-permute-start.7 = (bf16[4,1,128,256]{2,3,1,0:T(8,128)(2,1)S(1)}, bf16[4,1,128,256]{2,3,1,0:T(8,128)(2,1)S(1)}, u32[]{:S(2)}, u32[]{:S(2)}) collective-permute-start(bf16[4,1,128,256]{2,3,1,0:T(8,128)(2,1)S(1)} %get-tuple-element.69), channel_id=1, source_target_pairs={{1,0},{2,1},{3,2},{0,3},{5,4},{6,5},{7,6},{4,7},{9,8},{10,9},{11,1... | collective-permute-start | bytes 786440 | tf_op jit(solution)/shard_map/ppermute | solution.py:20
  683.3 8.4 %copy-start.1 = (bf16[4,64,64]{2,1,0:T(8,128)(2,1)S(1)}, bf16[4,64,64]{2,1,0:T(8,128)(2,1)}, u32[]{:S(2)}) copy-start(bf16[4,64,64]{2,1,0:T(8,128)(2,1)} %param.9) | copy-start | bytes 98308
  (55 other events, 224.7 us)
Sparse Core Ops, SparseCore 0:
  121.5 147.2 all-gather.2
  296.3 247.9 all-reduce.3
